TPU v7x, 256 devices: a whole 4x4x8 slice. The times are simulated.
256 devices in a mesh: view: 16 (over z, y_hi), row: 16 (over x, y_lo, core).
Axes of the slice: x: 4, y: 4 (y_hi: 2, y_lo: 2; y = y_hi * 2 + y_lo), z: 8, core: 2. Of those that a mesh axis runs over, the one named last changes fastest.
Arguments:
- latent: bfloat16 [1, 16, 32, 72, 1280], P(None, 'view', 'row'), may hold values from -30 to 30
- gn_gain: float32 [1280], replicated, may hold values from 0.25 to 1.75
- gn_bias: float32 [1280], replicated, may hold values from -3 to 3
- cam_idx: int32 [1, 16], P(None, 'view'), may hold values from 0 to 63
- noise_idx: int32 [1], replicated, may hold values from 0 to 999
- cam_table: bfloat16 [64, 2560], replicated, may hold values from -2 to 2
- noise_table: bfloat16 [1000, 2560], replicated, may hold values from -2 to 2
- conv_w: bfloat16 [3, 3, 1280, 1280], P(None, None, None, 'row'), may hold values from -0.0546875 to 0.0546875
- conv_bias: float32 [1280], replicated, may hold values from -3 to 3
- ln_gain: float32 [1280], replicated, may hold values from 0.25 to 1.75
- attn_in: bfloat16 [3, 1280, 1280], P(None, None, 'view'), may hold values from -0.15625 to 0.15625
- attn_out: bfloat16 [1280, 1280], P('view'), may hold values from -0.15625 to 0.15625
- head_scale: float32 [20], replicated, may hold values from 0.4 to 135
Outputs:
- block_out: bfloat16 [1, 16, 32, 72, 1280], P(None, 'view', 'row')
All inputs are finite; a program needn't handle non-finite values.
Results may differ from a plain program's by a relative error of at most 0.02.
Values may be sent and summed in bfloat16 or wider, within the bound.
No kernel may reach another device: no remote copies, remote signals or barrier semaphores. Data moves between devices by JAX's collectives and lax.ppermute only.
A program may use at most 192 MiB of HBM per device.

v0:
```python
import math
import jax
import jax.numpy as jnp
from jax import lax
from jax.sharding import PartitionSpec as P

GROUPS = 32
epsilon = 1e-05


def attend(query, key_block, value, head_scale):
    view_count = query.shape[0]
    item_count = query.shape[2]
    channels = query.shape[3]
    head_count = head_scale.shape[0]
    head_size = channels // head_count
    query_heads = query.reshape(view_count, item_count, head_count, head_size)
    key_heads = key_block.reshape(view_count, item_count, head_count, head_size)
    value_heads = value.reshape(view_count, item_count, head_count, head_size)
    scores = jnp.einsum(
        "vihd,uihd->ihvu", query_heads, key_heads, preferred_element_type=jnp.float32
    )
    scores = scores * (head_scale / math.sqrt(head_size))[None, :, None, None]
    peak_score = jnp.max(scores, axis=-1, keepdims=True)
    exp_scores = jnp.exp(scores - peak_score)
    soft_weights = (exp_scores / jnp.sum(exp_scores, axis=-1, keepdims=True)).astype(jnp.bfloat16)
    mixed = jnp.einsum(
        "ihvu,uihd->vihd", soft_weights, value_heads, preferred_element_type=jnp.float32
    )
    return mixed.astype(jnp.bfloat16).reshape(view_count, 1, item_count, channels)


def send_back(mixed):
    return lax.all_to_all(mixed, VIEW, split_axis=0, concat_axis=1, tiled=True)


def send_out(pixel_major):
    ys = lax.axis_size("vy")
    zs = lax.axis_size("vz")
    local_views = pixel_major.shape[0]
    parts = pixel_major.reshape((local_views, zs, ys) + pixel_major.shape[2:])
    parts = lax.all_to_all(parts, "vy", split_axis=2, concat_axis=0, tiled=True)
    parts = lax.all_to_all(parts, "vz", split_axis=1, concat_axis=1, tiled=True)
    parts = jnp.swapaxes(parts, 0, 1)
    return parts.reshape((zs * ys * local_views, 1) + pixel_major.shape[2:])


def local(
    latent,
    gn_gain,
    gn_bias,
    cam_idx,
    noise_idx,
    cam_table,
    noise_table,
    conv_w,
    conv_bias,
    ln_gain,
    attn_in,
    attn_out,
    head_scale,
):
    samples, local_views, local_rows, local_cols, channels = latent.shape
    width_out = ln_gain.shape[0]
    out_part = conv_w.shape[-1]
    whole = lax.all_gather(latent, ROW, axis=2, tiled=True)
    whole, attn_in = lax.optimization_barrier((whole, attn_in))
    core = lax.axis_index("core")
    half_in = attn_in.shape[1] // 2
    half_out = attn_out.shape[1] // 2
    in_half = lax.dynamic_slice_in_dim(attn_in, core * half_in, half_in, axis=1)
    in_half = lax.all_gather(in_half, VIEW, axis=0, tiled=False)
    out_half = lax.dynamic_slice_in_dim(attn_out, core * half_out, half_out, axis=1)
    view_devices = lax.axis_size(VIEW)
    out_half = jnp.broadcast_to(out_half[None], (view_devices,) + out_half.shape)
    out_half = lax.all_to_all(out_half, VIEW, split_axis=0, concat_axis=0, tiled=True)
    out_half = out_half.reshape(-1, half_out)
    all_rows = whole.shape[2]
    x_float = whole.astype(jnp.float32)
    grouped = x_float.reshape(
        samples, local_views, all_rows, local_cols, GROUPS, channels // GROUPS
    )
    average = jnp.mean(grouped, axis=(2, 3, 5), keepdims=True)
    centred = grouped - average
    variance = jnp.mean(centred * centred, axis=(2, 3, 5), keepdims=True)
    normed = (centred * lax.rsqrt(variance + epsilon)).reshape(x_float.shape)
    cam_film = jnp.take(cam_table, cam_idx, axis=0).astype(jnp.float32)
    noise_film = jnp.take(noise_table, noise_idx, axis=0).astype(jnp.float32)
    film_rows = cam_film + noise_film[:, None, :]
    film_scale = film_rows[:, :, None, None, :channels]
    film_shift = film_rows[:, :, None, None, channels:]
    hidden = (normed * gn_gain + gn_bias) * (1.0 + film_scale) + film_shift
    activated = jax.nn.silu(hidden).astype(jnp.bfloat16)
    out_half, activated = lax.optimization_barrier((out_half, activated))
    swap = [(0, 1), (1, 0)]
    out_other = lax.ppermute(out_half, "core", swap)
    taps = conv_w.shape[1]
    padded = jnp.pad(activated, ((0, 0), (0, 0), (1, 1), (0, 0), (0, 0)))
    tap_sum = None
    for tap_row in range(conv_w.shape[0]):
        rows_in = padded[:, :, tap_row : tap_row + all_rows].reshape(-1, channels)
        weight_row = jnp.transpose(conv_w[tap_row], (1, 0, 2)).reshape(channels, taps * out_part)
        part = jnp.dot(rows_in, weight_row, preferred_element_type=jnp.float32)
        tap_sum = part if tap_sum is None else tap_sum + part
    tap_sum = tap_sum.reshape(samples, local_views, all_rows, local_cols, taps, out_part)
    wide = jnp.pad(tap_sum, ((0, 0), (0, 0), (0, 0), (1, 1), (0, 0), (0, 0)))
    conv_out = (
        wide[:, :, :, 0:local_cols, 0]
        + wide[:, :, :, 1 : local_cols + 1, 1]
        + wide[:, :, :, 2 : local_cols + 2, 2]
    )
    me = lax.axis_index("chip") * lax.axis_size("core") + core
    conv_part = conv_out.astype(jnp.bfloat16)
    conv_rows = lax.all_to_all(conv_part, ROW, split_axis=2, concat_axis=4, tiled=True)
    out_other, conv_rows = lax.optimization_barrier((out_other, conv_rows))
    resid_out = (latent.astype(jnp.float32) + conv_rows.astype(jnp.float32) + conv_bias).astype(
        jnp.bfloat16
    )
    resid_float = resid_out.astype(jnp.float32)
    middle = jnp.mean(resid_float, axis=-1, keepdims=True)
    spread_y = jnp.mean((resid_float - middle) ** 2, axis=-1, keepdims=True)
    normed_y = ((resid_float - middle) * lax.rsqrt(spread_y + epsilon) * ln_gain).astype(
        jnp.bfloat16
    )
    view_devices = lax.axis_size(VIEW)
    per_device = samples * local_rows * local_cols // view_devices
    pixel_major = jnp.moveaxis(normed_y, 1, 0).reshape(
        local_views, view_devices, per_device, width_out
    )
    views = send_out(pixel_major)
    in_half, views = lax.optimization_barrier((in_half, views))
    in_other = lax.ppermute(in_half, "core", swap)
    flat_block = views.reshape(-1, width_out)
    block_mine = lax.dynamic_slice_in_dim(flat_block, core * half_in, half_in, axis=1)
    block_other = lax.dynamic_slice_in_dim(flat_block, (1 - core) * half_in, half_in, axis=1)
    triple_in = jnp.einsum(
        "pc,jmcd->mpjd", block_mine, in_half, preferred_element_type=jnp.float32
    ) + jnp.einsum("pc,jmcd->mpjd", block_other, in_other, preferred_element_type=jnp.float32)
    triple_in = triple_in.astype(jnp.bfloat16).reshape((3,) + views.shape)
    mixed = send_back(attend(triple_in[0], triple_in[1], triple_in[2], head_scale))
    mixed = jnp.moveaxis(
        mixed.reshape(local_views, samples, local_rows, local_cols, width_out), 0, 1
    )
    flat_mixed = mixed.reshape(-1, width_out)
    cols_mine = jnp.dot(flat_mixed, out_half, preferred_element_type=jnp.float32)
    cols_other = jnp.dot(flat_mixed, out_other, preferred_element_type=jnp.float32)
    projected = jnp.where(
        core == 0,
        jnp.concatenate([cols_mine, cols_other], axis=1),
        jnp.concatenate([cols_other, cols_mine], axis=1),
    )
    return (resid_float + projected.reshape(resid_float.shape)).astype(jnp.bfloat16)


ROW = ("chip", "core")
VIEW = ("vz", "vy")


def solution(mesh):
    cores = 2
    split = jax.sharding.Mesh(
        mesh.devices.reshape(mesh.shape["view"] // 2, 2, mesh.shape["row"] // cores, cores),
        ("vz", "vy", "chip", "core"),
    )
    placed = (
        P(None, VIEW, ROW, None, None),
        P(),
        P(),
        P(None, VIEW),
        P(),
        P(),
        P(),
        P(None, None, None, ROW),
        P(),
        P(),
        P(None, None, VIEW),
        P(VIEW, None),
        P(),
    )
    return jax.shard_map(
        local,
        mesh=split,
        in_specs=placed,
        out_specs=P(None, VIEW, ROW, None, None),
        check_vma=False,
    )
```

profile of v0, /device:TPU:2, one launch (start us, length us, event | category | flops | bytes accessed | tf_op | source)
XLA Modules:
  0.0 250.4 jit_solution(865494250867244917)
XLA Ops:
  9.5 11.2 %all-to-all-start = ((bf16[16,80,640]{2,1,0:T(8,128)(2,1)}), bf16[16,80,640]{2,1,0:T(8,128)(2,1)}, u32[]{:S(2)}, u32[]{:S(2)}) async-start(bf16[16,80,640]{2,1,0:T(8,128)(2,1)} %broadcast_in_dim.26), calls=%async_computation | async-start | bytes 3276800 | tf_op jit(solution)/shard_map/all_to_all | solution.py:76
  24.8 45.9 %all-gather.4.cloned.1.call-done = bf16[1,1,32,72,1280]{4,3,1,0,2:T(8,128)(2,1)} async-done(((bf16[1,1,2,72,1280]{4,3,1,0,2:T(8,128)(2,1)}), bf16[1,1,32,72,1280]{4,3,1,0,2:T(8,128)(2,1)}) %all-gather.4.cloned.1.call-update) | async-done | bytes 5898256 | tf_op jit(solution)/shard_map/all_gather | solution.py:66
  70.6 3.5 %convert_reduce_fusion = f32[1280]{0:T(1024)S(1)} fusion(bf16[1,1,32,72,1280]{4,3,1,0,2:T(8,128)(2,1)} %all-gather.4.cloned.1.call-done), kind=kLoop, calls=%fused_computation.2 | loop fusion | flops 5896960 | bytes 5903360 | tf_op jit(solution)/shard_map/reduce_sum | solution.py:83
  75.4 4.3 %fusion.3 = f32[1280]{0:T(1024)S(1)} fusion(bf16[1,1,32,72,1280]{4,3,1,0,2:T(8,128)(2,1)} %all-gather.4.cloned.1.call-done, f32[1280]{0:T(1024)S(1)} %sub.42), kind=kLoop, calls=%fused_computation.5 | loop fusion | flops 11795200 | bytes 5908480 | tf_op jit(solution)/shard_map/reduce_sum | solution.py:85
  80.0 8.4 %multiply_convert_fusion = bf16[1,1,32,72,1280]{4,3,1,0,2:T(8,128)(2,1)} fusion(bf16[1,1,32,72,1280]{4,3,1,0,2:T(8,128)(2,1)} %all-gather.4.cloned.1.call-done, f32[1280]{0:T(1024)S(1)} %get-tuple-element.44, f32[1280]{0:T(1024)S(1)} %get-tuple-element.43, f32[1280]{0:T(1024)S(1)} %copy-done.6, f32[1280]{0:T(1024)S(1)} %copy-done.7, f32[1280]{0:T(1024)S(1)} %mul.83, ...), kind=kLoop, calls=%fused_computation.10 | loop fusion | flops 35389440 | bytes 11827200 | tf_op jit(solution)/shard_map/convert_element_type | solution.py:93
  88.6 5.0 %pad_slice_fusion = (bf16[1,1,32,72,1280]{4,3,1,0,2:T(8,128)(2,1)S(1)}, bf16[1,1,32,72,1280]{4,3,1,0,2:T(8,128)(2,1)S(1)}) fusion(bf16[1,1,32,72,1280]{4,3,1,0,2:T(8,128)(2,1)} %multiply_convert_fusion), kind=kLoop, calls=%fused_computation.11 | loop fusion | bytes 17694720 | tf_op jit(solution)/shard_map/slice | solution.py:101
  96.4 1.8 convolution_add_fusion.1
  99.9 5.2 %reshape.304 = f32[1,1,32,72,3,80]{3,2,5,4,1,0:T(8,128)} reshape(f32[2304,240]{0,1:T(8,128)S(1)} %convolution_add_fusion) | data formatting | bytes 4423680 | tf_op jit(solution)/shard_map/reshape | solution.py:105
  105.2 2.9 %fusion.35 = bf16[1,1,32,72,80]{3,2,4,1,0:T(8,128)(2,1)S(1)} fusion(f32[1,1,32,72,3,80]{3,2,5,4,1,0:T(8,128)} %reshape.304), kind=kLoop, calls=%fused_computation.49 | loop fusion | flops 552960 | bytes 5611520 | tf_op jit(solution)/shard_map/convert_element_type | solution.py:113
  108.9 14.5 %all_to_all.55 = bf16[1,1,32,72,80]{4,3,1,0,2:T(8,128)(2,1)S(1)} all-to-all(bf16[1,1,32,72,80]{4,3,1,0,2:T(8,128)(2,1)S(1)} %copy.57), channel_id=1, replica_groups=mesh['vz'=8,'vy'=2,'chip'=8,'core'=2] {'chip','core'}, dimensions={2} | all-to-all | bytes 737280 | tf_op jit(solution)/shard_map/all_to_all | solution.py:114
  125.3 16.8 %all_to_all.56 = bf16[1,8,2,9,1280]{4,1,3,0,2:T(8,128)(2,1)S(1)} all-to-all(bf16[1,8,2,9,1280]{4,1,3,0,2:T(8,128)(2,1)S(1)} %copy.59), channel_id=1, replica_groups=mesh['vz'=8,'vy'=2,'chip'=8,'core'=2] {'vy'}, dimensions={2} | all-to-all | bytes 737280 | tf_op jit(solution)/shard_map/all_to_all | solution.py:42
  142.5 21.6 %all_to_all.57 = bf16[2,8,1,9,1280]{4,0,3,2,1:T(2,128)(2,1)S(1)} all-to-all(bf16[2,8,1,9,1280]{4,0,3,2,1:T(2,128)(2,1)S(1)} %copy.60), channel_id=1, replica_groups=mesh['vz'=8,'vy'=2,'chip'=8,'core'=2] {'vz'}, dimensions={1} | all-to-all | bytes 737280 | tf_op jit(solution)/shard_map/all_to_all | solution.py:43
  164.5 20.6 %all-gather.6.cloned.1.call-done = bf16[48,640,80]{1,2,0:T(8,128)(2,1)} async-done(((bf16[3,640,80]{1,2,0:T(8,128)(2,1)}), bf16[48,640,80]{1,2,0:T(8,128)(2,1)}) %all-gather.6.cloned.1.call-update) | async-done | bytes 4915216 | tf_op jit(solution)/shard_map/all_gather | solution.py:72
  185.4 5.1 %fusion.37 = f32[16,3,80,144]{2,3,1,0:T(8,128)S(1)} fusion(bf16[16,3,640,80]{2,3,1,0:T(8,128)(2,1)} %bitcast.96, bf16[144,1280]{1,0:T(8,128)(2,1)S(1)} %reshape.306, s32[]{:T(128)S(6)} %select_n.60), kind=kOutput, calls=%fused_computation.52 | convolution fusion | flops 707788800 | bytes 7311364 | tf_op jit(solution)/shard_map/pc,jmcd->mpjd/dot_general | solution.py:136
  190.5 3.1 %collective-permute-done.1 = bf16[16,3,640,80]{2,3,1,0:T(8,128)(2,1)} collective-permute-done((bf16[16,3,640,80]{2,3,1,0:T(8,128)(2,1)}, bf16[16,3,640,80]{2,3,1,0:T(8,128)(2,1)}, u32[]{:S(2)}, u32[]{:S(2)}) %collective-permute-start.1) | collective-permute-done | bytes 4915232 | tf_op jit(solution)/shard_map/ppermute | solution.py:132
  193.7 5.1 %fusion.13 = bf16[3,144,16,80]{3,1,0,2:T(8,128)(2,1)S(1)} fusion(f32[16,3,80,144]{2,3,1,0:T(8,128)S(1)} %fusion.37, bf16[16,3,640,80]{2,3,1,0:T(8,128)(2,1)} %collective-permute-done.1, bf16[144,1280]{1,0:T(8,128)(2,1)S(1)} %reshape.306, s32[]{:T(128)S(6)} %select_n.66), kind=kOutput, calls=%fused_computation.23 | convolution fusion | flops 708894720 | bytes 9744388 | tf_op jit(solution)/shard_map/pc,jmcd->mpjd/dot_general | solution.py:138
  200.4 2.2 reshape_squeeze.11
  202.8 2.2 reshape_squeeze.9
  205.0 3.2 %fusion.54 = (f32[9,20,16]{2,1,0:T(8,128)S(1)}, f32[9,20,16,16]{2,3,1,0:T(8,128)}) fusion(bf16[16,9,20,64]{3,2,1,0:T(8,128)(2,1)} %reshape_squeeze.11, bf16[16,9,20,64]{3,2,1,0:T(8,128)(2,1)S(1)} %reshape_squeeze.10, f32[20]{0:T(128)S(1)} %broadcast_multiply_fusion.1), kind=kOutput, calls=%fused_computation.76 | convolution fusion | flops 6036495 | bytes 933200 | tf_op jit(solution)/shard_map/sub | solution.py:25
  208.1 2.1 fusion.18
  211.9 4.6 %all-to-all-start.4 = ((bf16[16,1,9,1280]{3,2,1,0:T(8,128)(2,1)}), bf16[16,1,9,1280]{3,2,1,0:T(8,128)(2,1)S(1)}, u32[]{:S(2)}, u32[]{:S(2)}) async-start(bf16[16,1,9,1280]{3,2,1,0:T(8,128)(2,1)} %reshape.372), calls=%async_computation.4 | async-start | bytes 1310720 | tf_op jit(solution)/shard_map/all_to_all | solution.py:34
  216.5 22.1 %all-to-all-done.4 = bf16[16,1,9,1280]{3,2,1,0:T(8,128)(2,1)S(1)} async-done(((bf16[16,1,9,1280]{3,2,1,0:T(8,128)(2,1)}), bf16[16,1,9,1280]{3,2,1,0:T(8,128)(2,1)S(1)}, u32[]{:S(2)}, u32[]{:S(2)}) %all-to-all-start.4) | async-done | bytes 368672 | tf_op jit(solution)/shard_map/all_to_all | solution.py:34
  238.8 1.9 fusion.19
  240.7 1.9 fusion.22
  (69 shorter events, 20.0 us)
Async XLA Ops:
  6.5 67.7 %copy-start = (bf16[3,1280,80]{1,2,0:T(8,128)(2,1)S(1)}, bf16[3,1280,80]{1,2,0:T(8,128)(2,1)}, u32[]{:S(2)}) copy-start(bf16[3,1280,80]{1,2,0:T(8,128)(2,1)} %param.23) | copy-start | bytes 1843204
  6.5 64.1 %all-gather.4.cloned.1.call-start = ((), (), s32[]{:S(2)}) async-start(), calls=%async_computation.5 | async-start | bytes 6266880 | tf_op jit(solution)/shard_map/all_gather | solution.py:66
  9.5 78.9 %all-to-all-start = ((bf16[16,80,640]{2,1,0:T(8,128)(2,1)}), bf16[16,80,640]{2,1,0:T(8,128)(2,1)}, u32[]{:S(2)}, u32[]{:S(2)}) async-start(bf16[16,80,640]{2,1,0:T(8,128)(2,1)} %broadcast_in_dim.26), calls=%async_computation | async-start | bytes 3276800 | tf_op jit(solution)/shard_map/all_to_all | solution.py:76
  20.7 164.4 %all-gather.6.cloned.1.call-start = ((), (), s32[]{:S(2)}) async-start(), calls=%async_computation.6 | async-start | bytes 5222400 | tf_op jit(solution)/shard_map/all_gather | solution.py:72
  74.2 5.8 %copy-start.6 = (f32[1280]{0:T(1024)S(1)}, f32[1280]{0:T(1024)}, u32[]{:S(2)}) copy-start(f32[1280]{0:T(1024)} %param.15) | copy-start | bytes 15364
  74.2 5.8 %copy-start.7 = (f32[1280]{0:T(1024)S(1)}, f32[1280]{0:T(1024)}, u32[]{:S(2)}) copy-start(f32[1280]{0:T(1024)} %param.14) | copy-start | bytes 15364
  88.4 35.7 %collective-permute-start = (bf16[1280,640]{1,0:T(8,128)(2,1)}, bf16[1280,640]{1,0:T(8,128)(2,1)}, u32[]{:S(2)}, u32[]{:S(2)}) collective-permute-start(bf16[1280,640]{1,0:T(8,128)(2,1)} %bitcast), channel_id=1, source_target_pairs={{0,1},{1,0},{2,3},{3,2},{4,5},{5,4},{6,7},{7,6},{8,9},{9,8},{10,11... | collective-permute-start | bytes 4915208 | tf_op jit(solution)/shard_map/ppermute | solution.py:96
  93.7 2.7 %copy-start.2 = (bf16[1,1,32,72,1280]{4,3,1,0,2:T(8,128)(2,1)S(1)}, bf16[1,1,32,72,1280]{4,3,1,0,2:T(8,128)(2,1)}, u32[]{:S(2)}) copy-start(bf16[1,1,32,72,1280]{4,3,1,0,2:T(8,128)(2,1)} %multiply_convert_fusion) | copy-start | bytes 17694724
  105.2 18.9 %copy-start.3 = (bf16[1,1,2,72,1280]{4,3,2,1,0:T(8,128)(2,1)S(1)}, bf16[1,1,2,72,1280]{4,3,2,1,0:T(8,128)(2,1)}, u32[]{:S(2)}) copy-start(bf16[1,1,2,72,1280]{4,3,2,1,0:T(8,128)(2,1)} %param.13) | copy-start | bytes 1105924
  105.2 18.9 %copy-start.4 = (f32[1280]{0:T(1024)S(1)}, f32[1280]{0:T(1024)}, u32[]{:S(2)}) copy-start(f32[1280]{0:T(1024)} %param.21) | copy-start | bytes 15364
  105.2 19.5 %copy-start.5 = (f32[1280]{0:T(1024)S(1)}, f32[1280]{0:T(1024)}, u32[]{:S(2)}) copy-start(f32[1280]{0:T(1024)} %param.22) | copy-start | bytes 15364
  123.4 61.7 %copy-start.8 = (f32[20]{0:T(128)S(1)}, f32[20]{0:T(128)}, u32[]{:S(2)}) copy-start(f32[20]{0:T(128)} %param.25) | copy-start | bytes 244
  185.1 8.5 %collective-permute-start.1 = (bf16[16,3,640,80]{2,3,1,0:T(8,128)(2,1)}, bf16[16,3,640,80]{2,3,1,0:T(8,128)(2,1)}, u32[]{:S(2)}, u32[]{:S(2)}) collective-permute-start(bf16[16,3,640,80]{2,3,1,0:T(8,128)(2,1)} %bitcast.95), channel_id=1, source_target_pairs={{0,1},{1,0},{2,3},{3,2},{4,5},{5,4},{6,7},{7,6},{8,9},{9,8},{10,11... | collective-permute-start | bytes 14745608 | tf_op jit(solution)/shard_map/ppermute | solution.py:132
  210.2 33.3 %copy-start.1 = (bf16[3,1280,80]{1,2,0:T(8,128)(2,1)S(1)}, bf16[3,1280,80]{1,2,0:T(8,128)(2,1)}, u32[]{:S(2)}) copy-start(bf16[3,1280,80]{1,2,0:T(8,128)(2,1)} %param.23) | copy-start | bytes 1843204
  211.9 26.7 %all-to-all-start.4 = ((bf16[16,1,9,1280]{3,2,1,0:T(8,128)(2,1)}), bf16[16,1,9,1280]{3,2,1,0:T(8,128)(2,1)S(1)}, u32[]{:S(2)}, u32[]{:S(2)}) async-start(bf16[16,1,9,1280]{3,2,1,0:T(8,128)(2,1)} %reshape.372), calls=%async_computation.4 | async-start | bytes 1310720 | tf_op jit(solution)/shard_map/all_to_all | solution.py:34
Sparse Core Ops, SparseCore 0:
  9.2 61.3 all-gather.3
  75.2 109.8 all-gather.5
where the time goes:
time: 251 us; the launch traced here: 250 us
  waiting for transfers between devices  92.5 us (37%)
  blocking collectives  53 us (21%)
  local copies, waits for them, and re-layouts  27.4 us (11%)
  matrix products  24.5 us (10%)
  other arithmetic  21.8 us (9%)
  starting transfers between devices  16.1 us (6%)
  between operations  15.1 us (6%)
    all_gather x1, waiting for transfers between devices, local(): whole = lax.all_gather(latent, ROW, axis=2, tiled=True)  45.9 us
    all_to_all x1, waiting for transfers between devices, send_back(): return lax.all_to_all(mixed, VIEW, split_axis=0, concat_axis=1, tiled=True)  22.1 us
    all_to_all x1, blocking collectives, send_out(): parts = lax.all_to_all(parts, 'vz', split_axis=1, concat_axis=1, tiled=True)  21.6 us
    all_gather x1, waiting for transfers between devices, local(): in_half = lax.all_gather(in_half, VIEW, axis=0, tiled=False)  20.6 us
    all_to_all x1, blocking collectives, send_out(): parts = lax.all_to_all(parts, 'vy', split_axis=2, concat_axis=0, tiled=True)  16.8 us
    all_to_all x1, blocking collectives, local(): lax.all_to_all(conv_part, ROW, split_axis=2, concat_axis=4, tiled=True)  14.5 us
    all_to_all x1, starting transfers between devices, local(): lax.all_to_all(out_half, VIEW, split_axis=0, concat_axis=0, tiled=True)  11.2 us
    convert_element_type x1, other arithmetic, local(): activated = jax.nn.silu(hidden).astype(jnp.bfloat16)  8.36 us
  transfers between devices with their start and end apart: 6, of which 4 were waited for; matrix products, arithmetic and copies ran while one was open for 20% of the time, Pallas kernels for 0%

commit v1 on v0

--- a/solution.py
+++ b/solution.py
@@ -6,6 +6,9 @@
 
 GROUPS = 32
 epsilon = 1e-05
+kinds_pair = lambda xs, axis_name: jnp.concatenate(
+    lax.all_to_all(jnp.stack([xs for _ in range(lax.psum(1, axis_name))]), axis_name, 0, 0), axis=2
+)
 
 
 def attend(query, key_block, value, head_scale):
@@ -63,7 +66,7 @@
     samples, local_views, local_rows, local_cols, channels = latent.shape
     width_out = ln_gain.shape[0]
     out_part = conv_w.shape[-1]
-    whole = lax.all_gather(latent, ROW, axis=2, tiled=True)
+    whole = kinds_pair(latent, ROW)
     whole, attn_in = lax.optimization_barrier((whole, attn_in))
     core = lax.axis_index("core")
     half_in = attn_in.shape[1] // 2

time: 251 us -> 321 us (1.28)
  waiting for transfers between devices: 92.5 us -> 127 us
  blocking collectives: 53 us -> 79.7 us
  starting transfers between devices: 16.1 us -> 21.7 us
    all_to_all x0 -> x1, waiting for transfers between devices: none -> 63.2 us  [lax.all_to_all(jnp.stack([xs for _ in range(lax.psum(1, axis_name))]), ax...]
    all_gather x1 -> x0, waiting for transfers between devices: 45.9 us -> none  [local(): whole = lax.all_gather(latent, ROW, axis=2, tiled=True)]
    all_to_all x1, blocking collectives: 14.5 us -> 42.9 us  [local(): lax.all_to_all(conv_part, ROW, split_axis=2, concat_axis=4, tiled=True)]
    all_to_all x1, waiting for transfers between devices: 0.01 us -> 24.5 us  [local(): lax.all_to_all(out_half, VIEW, split_axis=0, concat_axis=0, tiled=True)]
    all_gather x1, waiting for transfers between devices: 20.6 us -> 13.7 us  [local(): in_half = lax.all_gather(in_half, VIEW, axis=0, tiled=False)]
    all_to_all x0 -> x1, starting transfers between devices: none -> 6.76 us  [lax.all_to_all(jnp.stack([xs for _ in range(lax.psum(1, axis_name))]), ax...]
    another operation x1 -> x2, local copies, waits for them, and re-layouts: 0.17 us -> 4.17 us  [the longest x1 4 us: jnp.stack([xs for _ in range(lax.psum(1, axis_name))])]
  transfers between devices with their start and end apart: 6 -> 6, of which waited for: 4 -> 5; matrix products, arithmetic and copies ran while one was open for 20% -> 15% of each run, Pallas kernels for 0% -> 0%
where the time goes in v1:
time: 321 us; the launch traced here: 320 us
  waiting for transfers between devices  127 us (40%)
  blocking collectives  79.7 us (25%)
  local copies, waits for them, and re-layouts  30.2 us (9%)
  matrix products  24.5 us (8%)
  other arithmetic  21.8 us (7%)
  starting transfers between devices  21.7 us (7%)
  between operations  15.1 us (5%)
    all_to_all x1, waiting for transfers between devices, lax.all_to_all(jnp.stack([xs for _ in range(lax.psum(1, axis_name))]), ax...  63.2 us
    all_to_all x1, blocking collectives, local(): lax.all_to_all(conv_part, ROW, split_axis=2, concat_axis=4, tiled=True)  42.9 us
    all_to_all x1, waiting for transfers between devices, local(): lax.all_to_all(out_half, VIEW, split_axis=0, concat_axis=0, tiled=True)  24.5 us
    all_to_all x1, waiting for transfers between devices, send_back(): return lax.all_to_all(mixed, VIEW, split_axis=0, concat_axis=1, tiled=True)  22.1 us
    all_to_all x1, blocking collectives, send_out(): parts = lax.all_to_all(parts, 'vz', split_axis=1, concat_axis=1, tiled=True)  21.3 us
    all_to_all x1, blocking collectives, send_out(): parts = lax.all_to_all(parts, 'vy', split_axis=2, concat_axis=0, tiled=True)  15.5 us
    all_gather x1, waiting for transfers between devices, local(): in_half = lax.all_gather(in_half, VIEW, axis=0, tiled=False)  13.7 us
    all_to_all x1, starting transfers between devices, local(): lax.all_to_all(out_half, VIEW, split_axis=0, concat_axis=0, tiled=True)  10.2 us
  transfers between devices with their start and end apart: 6, of which 5 were waited for; matrix products, arithmetic and copies ran while one was open for 15% of the time, Pallas kernels for 0%

profile of v1, /device:TPU:2, one launch (start us, length us, event | category | flops | bytes accessed | tf_op | source)
XLA Modules:
  0.0 319.7 jit_solution(14160330490361481136)
XLA Ops:
  6.5 4.0 %stack.2 = bf16[16,1,1,2,72,1280]{5,4,3,2,1,0:T(8,128)(2,1)} broadcast(bf16[2,72,1280]{2,1,0:T(8,128)(2,1)} %bitcast.103), dimensions={3,4,5} | broadcast | bytes 6266880 | tf_op jit(solution)/shard_map/stack | solution.py:10
  10.5 6.8 %all-to-all-start.1 = ((bf16[16,1,1,2,72,1280]{5,4,3,2,1,0:T(8,128)(2,1)}), bf16[16,1,1,2,72,1280]{5,4,3,2,1,0:T(8,128)(2,1)}, u32[]{:S(2)}, u32[]{:S(2)}) async-start(bf16[16,1,1,2,72,1280]{5,4,3,2,1,0:T(8,128)(2,1)} %stack.2), calls=%async_computation.1 | async-start | bytes 11796480 | tf_op jit(solution)/shard_map/all_to_all | solution.py:10
  21.1 63.2 %all-to-all-done.1 = bf16[16,1,1,2,72,1280]{5,4,3,2,1,0:T(8,128)(2,1)} async-done(((bf16[16,1,1,2,72,1280]{5,4,3,2,1,0:T(8,128)(2,1)}), bf16[16,1,1,2,72,1280]{5,4,3,2,1,0:T(8,128)(2,1)}, u32[]{:S(2)}, u32[]{:S(2)}) %all-to-all-start.1) | async-done | bytes 5898272 | tf_op jit(solution)/shard_map/all_to_all | solution.py:10
  85.6 10.2 %all-to-all-start = ((bf16[16,80,640]{2,1,0:T(8,128)(2,1)}), bf16[16,80,640]{2,1,0:T(8,128)(2,1)}, u32[]{:S(2)}, u32[]{:S(2)}) async-start(bf16[16,80,640]{2,1,0:T(8,128)(2,1)} %broadcast_in_dim.26), calls=%async_computation | async-start | bytes 3276800 | tf_op jit(solution)/shard_map/all_to_all | solution.py:79
  95.9 3.5 %convert_reduce_fusion = f32[1280]{0:T(1024)S(1)} fusion(bf16[1,1,32,72,1280]{4,3,2,1,0:T(8,128)(2,1)} %bitcast.2), kind=kLoop, calls=%fused_computation.2 | loop fusion | flops 5896960 | bytes 5903360 | tf_op jit(solution)/shard_map/reduce_sum | solution.py:86
  100.6 4.3 %fusion.3 = f32[1280]{0:T(1024)S(1)} fusion(bf16[1,1,32,72,1280]{4,3,2,1,0:T(8,128)(2,1)} %bitcast.2, f32[1280]{0:T(1024)S(1)} %sub.42), kind=kLoop, calls=%fused_computation.5 | loop fusion | flops 11795200 | bytes 5908480 | tf_op jit(solution)/shard_map/reduce_sum | solution.py:88
  105.2 8.4 %multiply_convert_fusion = bf16[1,1,32,72,1280]{4,3,2,1,0:T(8,128)(2,1)} fusion(bf16[1,1,32,72,1280]{4,3,2,1,0:T(8,128)(2,1)} %bitcast.2, f32[1280]{0:T(1024)S(1)} %get-tuple-element.44, f32[1280]{0:T(1024)S(1)} %get-tuple-element.43, f32[1280]{0:T(1024)S(1)} %copy-done.7, f32[1280]{0:T(1024)S(1)} %copy-done.8, f32[1280]{0:T(1024)S(1)} %mul.83, f32[1280]{0:T(1024)S(1)} %sub.42), kind=kLoop, calls=%fused_computation.10 | loop fusion | flops 35389440 | bytes 11827200 | tf_op jit(solution)/shard_map/convert_element_type | solution.py:96
  113.6 24.5 %all-to-all-done = bf16[16,80,640]{2,1,0:T(8,128)(2,1)} async-done(((bf16[16,80,640]{2,1,0:T(8,128)(2,1)}), bf16[16,80,640]{2,1,0:T(8,128)(2,1)}, u32[]{:S(2)}, u32[]{:S(2)}) %all-to-all-start) | async-done | bytes 1638432 | tf_op jit(solution)/shard_map/all_to_all | solution.py:79
  138.1 5.0 %pad_slice_fusion = (bf16[1,1,32,72,1280]{4,3,2,1,0:T(8,128)(2,1)S(1)}, bf16[1,1,32,72,1280]{4,3,2,1,0:T(8,128)(2,1)S(1)}) fusion(bf16[1,1,32,72,1280]{4,3,2,1,0:T(8,128)(2,1)} %multiply_convert_fusion), kind=kLoop, calls=%fused_computation.11 | loop fusion | bytes 17694720 | tf_op jit(solution)/shard_map/slice | solution.py:104
  149.4 5.2 %reshape.311 = f32[1,1,32,72,3,80]{3,2,5,4,1,0:T(8,128)} reshape(f32[2304,240]{0,1:T(8,128)S(1)} %convolution_add_fusion) | data formatting | bytes 4423680 | tf_op jit(solution)/shard_map/reshape | solution.py:108
  154.7 2.9 fusion.35
  158.3 42.9 %all_to_all.60 = bf16[1,1,32,72,80]{4,3,1,0,2:T(8,128)(2,1)S(1)} all-to-all(bf16[1,1,32,72,80]{4,3,1,0,2:T(8,128)(2,1)S(1)} %copy.69), channel_id=1, replica_groups=mesh['vz'=8,'vy'=2,'chip'=8,'core'=2] {'chip','core'}, dimensions={2} | all-to-all | bytes 737280 | tf_op jit(solution)/shard_map/all_to_all | solution.py:117
  203.2 15.5 %all_to_all.61 = bf16[1,8,2,9,1280]{4,1,3,0,2:T(8,128)(2,1)S(1)} all-to-all(bf16[1,8,2,9,1280]{4,1,3,0,2:T(8,128)(2,1)S(1)} %copy.71), channel_id=1, replica_groups=mesh['vz'=8,'vy'=2,'chip'=8,'core'=2] {'vy'}, dimensions={2} | all-to-all | bytes 737280 | tf_op jit(solution)/shard_map/all_to_all | solution.py:45
  218.9 21.3 %all_to_all.62 = bf16[2,8,1,9,1280]{4,0,3,2,1:T(2,128)(2,1)S(1)} all-to-all(bf16[2,8,1,9,1280]{4,0,3,2,1:T(2,128)(2,1)S(1)} %copy.72), channel_id=1, replica_groups=mesh['vz'=8,'vy'=2,'chip'=8,'core'=2] {'vz'}, dimensions={1} | all-to-all | bytes 737280 | tf_op jit(solution)/shard_map/all_to_all | solution.py:46
  240.6 13.7 %all-gather.3.cloned.1.call-done = bf16[48,640,80]{1,2,0:T(8,128)(2,1)} async-done(((bf16[3,640,80]{1,2,0:T(8,128)(2,1)}), bf16[48,640,80]{1,2,0:T(8,128)(2,1)}) %all-gather.3.cloned.1.call-update) | async-done | bytes 4915216 | tf_op jit(solution)/shard_map/all_gather | solution.py:75
  254.7 5.1 %fusion.37 = f32[16,3,80,144]{2,3,1,0:T(8,128)S(1)} fusion(bf16[16,3,640,80]{2,3,1,0:T(8,128)(2,1)} %bitcast.97, bf16[144,1280]{1,0:T(8,128)(2,1)S(1)} %reshape.313, s32[]{:T(128)S(6)} %select_n.60), kind=kOutput, calls=%fused_computation.52 | convolution fusion | flops 707788800 | bytes 7311364 | tf_op jit(solution)/shard_map/pc,jmcd->mpjd/dot_general | solution.py:139
  259.8 3.1 collective-permute-done.1
  262.9 5.1 %fusion.13 = bf16[3,144,16,80]{3,1,0,2:T(8,128)(2,1)S(1)} fusion(f32[16,3,80,144]{2,3,1,0:T(8,128)S(1)} %fusion.37, bf16[16,3,640,80]{2,3,1,0:T(8,128)(2,1)} %collective-permute-done.1, bf16[144,1280]{1,0:T(8,128)(2,1)S(1)} %reshape.313, s32[]{:T(128)S(6)} %select_n.66), kind=kOutput, calls=%fused_computation.23 | convolution fusion | flops 708894720 | bytes 9744388 | tf_op jit(solution)/shard_map/pc,jmcd->mpjd/dot_general | solution.py:141
  269.7 2.2 reshape_squeeze.11
  272.1 2.2 reshape_squeeze.9
  274.2 3.2 fusion.54
  277.4 2.1 fusion.18
  281.2 4.7 %all-to-all-start.5 = ((bf16[16,1,9,1280]{3,2,1,0:T(8,128)(2,1)}), bf16[16,1,9,1280]{3,2,1,0:T(8,128)(2,1)S(1)}, u32[]{:S(2)}, u32[]{:S(2)}) async-start(bf16[16,1,9,1280]{3,2,1,0:T(8,128)(2,1)} %reshape.379), calls=%async_computation.5 | async-start | bytes 1310720 | tf_op jit(solution)/shard_map/all_to_all | solution.py:37
  285.9 22.1 %all-to-all-done.5 = bf16[16,1,9,1280]{3,2,1,0:T(8,128)(2,1)S(1)} async-done(((bf16[16,1,9,1280]{3,2,1,0:T(8,128)(2,1)}), bf16[16,1,9,1280]{3,2,1,0:T(8,128)(2,1)S(1)}, u32[]{:S(2)}, u32[]{:S(2)}) %all-to-all-start.5) | async-done | bytes 368672 | tf_op jit(solution)/shard_map/all_to_all | solution.py:37
  (71 shorter events, 23.5 us)
Async XLA Ops:
  6.5 93.0 %copy-start = (bf16[3,1280,80]{1,2,0:T(8,128)(2,1)S(1)}, bf16[3,1280,80]{1,2,0:T(8,128)(2,1)}, u32[]{:S(2)}) copy-start(bf16[3,1280,80]{1,2,0:T(8,128)(2,1)} %param.23) | copy-start | bytes 1843204
  10.5 9.0 %copy-start.4 = (bf16[80,1280]{1,0:T(8,128)(2,1)S(1)}, bf16[80,1280]{1,0:T(8,128)(2,1)}, u32[]{:S(2)}) copy-start(bf16[80,1280]{1,0:T(8,128)(2,1)} %param.24) | copy-start | bytes 614404
  10.5 73.8 %all-to-all-start.1 = ((bf16[16,1,1,2,72,1280]{5,4,3,2,1,0:T(8,128)(2,1)}), bf16[16,1,1,2,72,1280]{5,4,3,2,1,0:T(8,128)(2,1)}, u32[]{:S(2)}, u32[]{:S(2)}) async-start(bf16[16,1,1,2,72,1280]{5,4,3,2,1,0:T(8,128)(2,1)} %stack.2), calls=%async_computation.1 | async-start | bytes 11796480 | tf_op jit(solution)/shard_map/all_to_all | solution.py:10
  85.6 52.5 %all-to-all-start = ((bf16[16,80,640]{2,1,0:T(8,128)(2,1)}), bf16[16,80,640]{2,1,0:T(8,128)(2,1)}, u32[]{:S(2)}, u32[]{:S(2)}) async-start(bf16[16,80,640]{2,1,0:T(8,128)(2,1)} %broadcast_in_dim.26), calls=%async_computation | async-start | bytes 3276800 | tf_op jit(solution)/shard_map/all_to_all | solution.py:79
  95.8 158.6 %all-gather.3.cloned.1.call-start = ((), (), s32[]{:S(2)}) async-start(), calls=%async_computation.6 | async-start | bytes 5222400 | tf_op jit(solution)/shard_map/all_gather | solution.py:75
  99.4 5.8 %copy-start.7 = (f32[1280]{0:T(1024)S(1)}, f32[1280]{0:T(1024)}, u32[]{:S(2)}) copy-start(f32[1280]{0:T(1024)} %param.15) | copy-start | bytes 15364
  99.4 5.8 %copy-start.8 = (f32[1280]{0:T(1024)S(1)}, f32[1280]{0:T(1024)}, u32[]{:S(2)}) copy-start(f32[1280]{0:T(1024)} %param.14) | copy-start | bytes 15364
  138.1 63.8 %collective-permute-start = (bf16[1280,640]{1,0:T(8,128)(2,1)}, bf16[1280,640]{1,0:T(8,128)(2,1)}, u32[]{:S(2)}, u32[]{:S(2)}) collective-permute-start(bf16[1280,640]{1,0:T(8,128)(2,1)} %bitcast), channel_id=1, source_target_pairs={{0,1},{1,0},{2,3},{3,2},{4,5},{5,4},{6,7},{7,6},{8,9},{9,8},{10,11... | collective-permute-start | bytes 4915208 | tf_op jit(solution)/shard_map/ppermute | solution.py:99
  143.1 2.7 copy-start.2
  154.7 47.3 %copy-start.3 = (bf16[1,1,2,72,1280]{4,3,2,1,0:T(8,128)(2,1)S(1)}, bf16[1,1,2,72,1280]{4,3,2,1,0:T(8,128)(2,1)}, u32[]{:S(2)}) copy-start(bf16[1,1,2,72,1280]{4,3,2,1,0:T(8,128)(2,1)} %param.13) | copy-start | bytes 1105924
  154.7 47.3 %copy-start.5 = (f32[1280]{0:T(1024)S(1)}, f32[1280]{0:T(1024)}, u32[]{:S(2)}) copy-start(f32[1280]{0:T(1024)} %param.21) | copy-start | bytes 15364
  154.7 47.8 %copy-start.6 = (f32[1280]{0:T(1024)S(1)}, f32[1280]{0:T(1024)}, u32[]{:S(2)}) copy-start(f32[1280]{0:T(1024)} %param.22) | copy-start | bytes 15364
  201.2 53.2 %copy-start.9 = (f32[20]{0:T(128)S(1)}, f32[20]{0:T(128)}, u32[]{:S(2)}) copy-start(f32[20]{0:T(128)} %param.25) | copy-start | bytes 244
  254.4 8.5 %collective-permute-start.1 = (bf16[16,3,640,80]{2,3,1,0:T(8,128)(2,1)}, bf16[16,3,640,80]{2,3,1,0:T(8,128)(2,1)}, u32[]{:S(2)}, u32[]{:S(2)}) collective-permute-start(bf16[16,3,640,80]{2,3,1,0:T(8,128)(2,1)} %bitcast.96), channel_id=1, source_target_pairs={{0,1},{1,0},{2,3},{3,2},{4,5},{5,4},{6,7},{7,6},{8,9},{9,8},{10,11... | collective-permute-start | bytes 14745608 | tf_op jit(solution)/shard_map/ppermute | solution.py:135
  279.5 33.4 %copy-start.1 = (bf16[3,1280,80]{1,2,0:T(8,128)(2,1)S(1)}, bf16[3,1280,80]{1,2,0:T(8,128)(2,1)}, u32[]{:S(2)}) copy-start(bf16[3,1280,80]{1,2,0:T(8,128)(2,1)} %param.23) | copy-start | bytes 1843204
  281.2 26.8 %all-to-all-start.5 = ((bf16[16,1,9,1280]{3,2,1,0:T(8,128)(2,1)}), bf16[16,1,9,1280]{3,2,1,0:T(8,128)(2,1)S(1)}, u32[]{:S(2)}, u32[]{:S(2)}) async-start(bf16[16,1,9,1280]{3,2,1,0:T(8,128)(2,1)} %reshape.379), calls=%async_computation.5 | async-start | bytes 1310720 | tf_op jit(solution)/shard_map/all_to_all | solution.py:37
Sparse Core Ops, SparseCore 0:
  100.4 153.9 all-gather.2
